TPU v7x, 128 devices: a whole 4x4x4 slice. The times are simulated.
128 devices in a mesh: req: 4 (over y), exp: 32 (over z, x, core).
Axes of the slice: x: 4, y: 4, z: 4, core: 2. Of those that a mesh axis runs over, the one named last changes fastest.
Arguments:
- states: bfloat16 [2, 16384, 1024], P(None, ('req', 'exp')), may hold values from -6 to 6
- lengths: int32 [128, 4], P(('req', 'exp')), may hold values from 1 to 64, 128 in all within a row
- targets: int32 [16384], P('req'), may hold values from 0 to 36863
- routes: int32 [2, 16384, 8], P(None, ('req', 'exp')), may hold values from 0 to 31, all different within a row; in each aligned block of 128 rows (0 to 127, 128 to 255, ..., all dimensions but the last counted through in order) at most 40 rows name the same one
- gate_probs: float32 [2, 16384, 8], P(None, ('req', 'exp')), may hold values from 0.02 to 0.4
- owners: int32 [512], P(('req', 'exp')), may hold values from 0 to 511, each once
- norm_gains: float32 [2, 3, 1024], replicated, may hold values from 0.25 to 1.75
- qkv_weight: bfloat16 [2, 1024, 2048], replicated, may hold values from -14 to 14
- out_weight: bfloat16 [2, 1024, 1024], replicated, may hold values from -0.1875 to 0.1875
- expert_in: bfloat16 [2, 32, 1024, 1024], P(None, 'exp'), may hold values from -0.1875 to 0.1875
- expert_down: bfloat16 [2, 32, 512, 1024], P(None, 'exp'), may hold values from -0.25 to 0.25
- vocab_head: bfloat16 [2, 36864, 1024], P(None, 'exp'), may hold values from -170 to 170
Outputs:
- token_logp: float32 [2, 16384], P(None, ('req', 'exp'))
- seq_totals: float32 [512], P(('req', 'exp'))
Inputs may be any that keep to these rules, and one draw needn't show every extreme that they name: `lengths`: each row sums to 128; some row reaches 64. `routes`: the 8 experts of a token are distinct; among the 128 tokens of one device, no expert is named by more than 40 of them for one model, and that bound is reached. `owners`: a permutation of the sequence numbers.
All inputs are finite; a program needn't handle non-finite values.
Results may differ from a plain program's by a relative error of at most 0.012.
The roundings to bfloat16 on the way count: a program that leaves them out, or rounds other values in their place, can miss the bound.
Values may be sent and summed in bfloat16 or wider, within the bound.
No kernel may reach another device: no remote copies, remote signals or barrier semaphores. Data moves between devices by JAX's collectives and lax.ppermute only.
A program may use at most 128 MiB of HBM per device.

v0:
```python
import jax
import jax.numpy as jnp
from jax import lax
from jax.sharding import PartitionSpec as P

HEADS = 16
KV_HEADS = 8
HEAD_DIM = 64
EXPERT_FF = 512
EXPERTS = 32
TOP = 8
CAP = 40
EPSILON = 1e-06
RESIDUAL_SCALE = 0.22
SCORE_SCALE = 0.015625
LOGIT_DIVISOR = 6.0
ROTARY_BASE = 10000.0


def combined_all(x, axis, combine):
    everything = jax.tree.map(lambda part: lax.all_gather(part, axis), x)
    initial = jax.tree.map(lambda part: part[0], everything)

    def step(k, so_far):
        return combine(so_far, jax.tree.map(lambda part: part[k], everything))

    return lax.fori_loop(1, lax.axis_size(axis), step, initial)


def root_norm(values, gain_row):
    values = values.astype(jnp.float32)
    scaled = lax.rsqrt(jnp.mean(values * values, axis=-1, keepdims=True) + EPSILON)
    return values * scaled * gain_row


def segment_table(length_row, token_count):
    seq_ends = jnp.cumsum(length_row)
    seq_starts = seq_ends - length_row
    places = jnp.arange(token_count, dtype=jnp.int32)
    segment = jnp.sum((places[:, None] >= seq_ends[None, :]).astype(jnp.int32), axis=1)
    member = segment[:, None] == jnp.arange(length_row.shape[0], dtype=jnp.int32)[None, :]
    position = places - jnp.sum(member.astype(jnp.int32) * seq_starts[None, :], axis=1)
    return (segment, member, position)


def rotary(values, position):
    half_dim = values.shape[-1] // 2
    frequency = ROTARY_BASE ** (-2.0 * jnp.arange(half_dim, dtype=jnp.float32) / values.shape[-1])
    angles = position.astype(jnp.float32)[:, None] * frequency[None, :]
    angles = jnp.concatenate([angles, angles], axis=-1)[:, None, :]
    leading = values[..., :half_dim]
    trailing = values[..., half_dim:]
    turned = jnp.concatenate([-trailing, leading], axis=-1)
    return values * jnp.cos(angles) + turned * jnp.sin(angles)


def attend(block_states, segment, position, gain_row, qkv_weight, out_weight):
    token_count = block_states.shape[0]
    group_size = HEADS // KV_HEADS
    normed = root_norm(block_states, gain_row).astype(jnp.bfloat16)
    mixed = jnp.dot(normed, qkv_weight, preferred_element_type=jnp.float32)
    queries = rotary(
        mixed[:, : HEADS * HEAD_DIM].reshape(token_count, HEADS, HEAD_DIM), position
    ).astype(jnp.bfloat16)
    keys_all = rotary(
        mixed[:, HEADS * HEAD_DIM : (HEADS + KV_HEADS) * HEAD_DIM].reshape(
            token_count, KV_HEADS, HEAD_DIM
        ),
        position,
    ).astype(jnp.bfloat16)
    values_all = (
        mixed[:, (HEADS + KV_HEADS) * HEAD_DIM :]
        .reshape(token_count, KV_HEADS, HEAD_DIM)
        .astype(jnp.bfloat16)
    )
    grouped = queries.reshape(token_count, KV_HEADS, group_size, HEAD_DIM)
    scores = (
        jnp.einsum("tgqd,sgd->gqts", grouped, keys_all, preferred_element_type=jnp.float32)
        * SCORE_SCALE
    )
    places = jnp.arange(token_count, dtype=jnp.int32)
    allowed = (segment[:, None] == segment[None, :]) & (places[None, :] <= places[:, None])
    scores = jnp.where(allowed, scores, -1e30)
    highest = jnp.max(scores, axis=-1, keepdims=True)
    weights = jnp.exp(scores - highest)
    weights = (weights / jnp.sum(weights, axis=-1, keepdims=True)).astype(jnp.bfloat16)
    attended = jnp.einsum(
        "gqts,sgd->tgqd", weights, values_all, preferred_element_type=jnp.float32
    ).astype(jnp.bfloat16)
    projected = jnp.dot(
        attended.reshape(token_count, HEADS * HEAD_DIM),
        out_weight,
        preferred_element_type=jnp.float32,
    )
    return (block_states.astype(jnp.float32) + RESIDUAL_SCALE * projected).astype(jnp.bfloat16)


def join_parts(first_part, second_part):
    first_max, first_mass, first_hit = first_part
    second_max, second_mass, second_hit = second_part
    joined_max = jnp.maximum(first_max, second_max)
    joined_mass = first_mass * jnp.exp(first_max - joined_max) + second_mass * jnp.exp(
        second_max - joined_max
    )
    return (joined_max, joined_mass, first_hit + second_hit)


def per_device(
    states,
    lengths,
    targets,
    routes,
    gate_probs,
    owners,
    norm_gains,
    qkv_weight,
    out_weight,
    expert_in,
    expert_down,
    vocab_head,
):
    token_count = states.shape[1]
    width = states.shape[2]
    segment, member, position = segment_table(lengths[0], token_count)
    residual = jnp.stack(
        [
            attend(
                states[which],
                segment,
                position,
                norm_gains[which, 0],
                qkv_weight[which],
                out_weight[which],
            )
            for which in range(2)
        ]
    )
    moe_in = root_norm(residual, norm_gains[:, 1][:, None, :]).astype(jnp.bfloat16)
    groups = lax.axis_size("exp")
    local_count = expert_in.shape[1]
    flat_routes = routes.reshape(2, token_count * TOP)
    onehot = (flat_routes[..., None] == jnp.arange(EXPERTS, dtype=jnp.int32)).astype(jnp.int32)
    rank_slot = jnp.sum((jnp.cumsum(onehot, axis=1) - 1) * onehot, axis=2)
    slot_index = (
        flat_routes * CAP + rank_slot + jnp.arange(2, dtype=jnp.int32)[:, None] * (EXPERTS * CAP)
    ).reshape(-1)
    token_index = jnp.arange(token_count * TOP, dtype=jnp.int32) // TOP
    outgoing = (
        jnp.zeros((2 * EXPERTS * CAP, width), jnp.bfloat16)
        .at[slot_index]
        .set(moe_in[:, token_index].reshape(-1, width))
    )
    arrived = lax.all_to_all(
        outgoing.reshape(2, groups, local_count * CAP, width),
        "exp",
        split_axis=1,
        concat_axis=1,
        tiled=True,
    )
    inputs = arrived.reshape(2, groups, local_count, CAP, width)
    gate_up = jnp.einsum("mslcd,mldf->mslcf", inputs, expert_in, preferred_element_type=jnp.float32)
    hidden = (jax.nn.silu(gate_up[..., :EXPERT_FF]) * gate_up[..., EXPERT_FF:]).astype(jnp.bfloat16)
    produced = jnp.einsum(
        "mslcf,mlfd->mslcd", hidden, expert_down, preferred_element_type=jnp.float32
    ).astype(jnp.bfloat16)
    returned = lax.all_to_all(
        produced.reshape(2, groups, local_count * CAP, width),
        "exp",
        split_axis=1,
        concat_axis=1,
        tiled=True,
    )
    picked = returned.reshape(2 * EXPERTS * CAP, width)[slot_index].reshape(
        2, token_count, TOP, width
    )
    mixture = jnp.sum(gate_probs[..., None] * picked.astype(jnp.float32), axis=2)
    final = root_norm(
        residual.astype(jnp.float32) + RESIDUAL_SCALE * mixture, norm_gains[:, 2][:, None, :]
    ).astype(jnp.bfloat16)
    shard = lax.axis_index("exp")
    vocab_rows = vocab_head.shape[1]
    lowest = shard * vocab_rows
    vocab_ids = jnp.arange(vocab_rows, dtype=jnp.int32)
    shard_piece = lax.all_gather(final, "exp", axis=1, tiled=True)
    piece_rows = shard_piece.shape[1]
    block_rows = 512
    block_count = piece_rows // block_rows
    wanted_all = targets - lowest

    def one_block(block_number):
        row_block = lax.dynamic_slice_in_dim(shard_piece, block_number * block_rows, block_rows, 1)
        wanted = lax.dynamic_slice_in_dim(wanted_all, block_number * block_rows, block_rows, 0)
        logits = (
            jnp.einsum("mtd,mvd->mtv", row_block, vocab_head, preferred_element_type=jnp.float32)
            / LOGIT_DIVISOR
        )
        highest = jnp.max(logits, axis=2)
        masses = jnp.sum(jnp.exp(logits - highest[..., None]), axis=2)
        chosen = jnp.sum(
            jnp.where(wanted[None, :, None] == vocab_ids[None, None, :], logits, 0.0), axis=2
        )
        return (highest, masses, chosen)

    block_max, block_mass, block_hit = lax.map(one_block, jnp.arange(block_count, dtype=jnp.int32))

    def place(fresh):
        ordered = jnp.transpose(fresh, (1, 0, 2)).reshape(2, piece_rows)
        return ordered

    part_max = place(block_max)
    part_mass = place(block_mass)
    part_hit = place(block_hit)
    all_max, all_mass, all_hit = combined_all((part_max, part_mass, part_hit), "exp", join_parts)
    begin = shard * token_count
    final_max = lax.dynamic_slice_in_dim(all_max, begin, token_count, 1)
    final_mass = lax.dynamic_slice_in_dim(all_mass, begin, token_count, 1)
    final_hit = lax.dynamic_slice_in_dim(all_hit, begin, token_count, 1)
    token_logp = final_hit - (final_max + jnp.log(final_mass))
    difference = token_logp[0] - token_logp[1]
    seq_sums = jnp.sum(member.astype(jnp.float32) * difference[:, None], axis=0)
    devices = lax.axis_size("req") * lax.axis_size("exp")
    everyone = devices * seq_sums.shape[0]
    dense_totals = jnp.sum(
        (owners[:, None] == jnp.arange(everyone, dtype=jnp.int32)[None, :]).astype(jnp.float32)
        * seq_sums[:, None],
        axis=0,
    )
    seq_totals = lax.psum_scatter(dense_totals, ("req", "exp"), scatter_dimension=0, tiled=True)
    return (token_logp, seq_totals)


def solution(mesh):
    in_specs = (
        P(None, ("req", "exp"), None),
        P(("req", "exp"), None),
        P("req"),
        P(None, ("req", "exp"), None),
        P(None, ("req", "exp"), None),
        P(("req", "exp")),
        P(),
        P(),
        P(),
        P(None, "exp", None, None),
        P(None, "exp", None, None),
        P(None, "exp", None),
    )
    out_specs = (P(None, ("req", "exp")), P(("req", "exp")))
    return jax.shard_map(
        per_device, mesh=mesh, in_specs=in_specs, out_specs=out_specs, check_vma=False
    )
```

profile of v0, /device:TPU:1, one launch (start us, length us, event | category | flops | bytes accessed | tf_op | source)
XLA Modules:
  0.0 671.6 jit_solution(7500306601122006520)
XLA Ops:
  9.4 3.1 fusion.15
  21.6 3.1 fusion.13
  41.6 2.8 convolution_convert_fusion.1
  47.5 15.8 %gather_fusion = bf16[1024,2,1024]{2,1,0:T(2,128)(2,1)} fusion(bf16[2,128,1024]{2,0,1:T(2,128)(2,1)S(1)} %copy.125, s32[1024]{0:T(1024)S(1)} %broadcast_clamp_fusion.1), kind=kCustom, calls=%fused_computation | custom fusion | bytes 8392704 | tf_op jit(solution)/shard_map/gather | solution.py:151
  63.3 5.6 copy.126
  68.9 18.0 %reduce-window.11 = s32[2,32,8,128]{3,2,1,0:T(8,128)S(1)} reduce-window(s32[2,32,8,128]{3,2,1,0:T(8,128)S(1)} %fusion.101, s32[]{:T(128)} %constant.119.clone.1), window={size=1x1x1x128 pad=0_0x0_0x0_0x127_0}, to_apply=%region_9.10 | reduce-window | flops 8323072 | bytes 524292 | tf_op jit(solution)/shard_map/reduce-window.1
  88.0 13.6 %scatter_custom_fusion = bf16[2560,1024]{1,0:T(8,128)(2,1)} fusion(s32[2048]{0:T(1024)S(1)} %bitcast.262, bf16[2048,1024]{1,0:T(8,128)(2,1)} %bitcast.240, bf16[]{:T(256)} %constant.129.clone.1), kind=kCustom, calls=%fused_computation.37 | custom fusion | bytes 5243392 | tf_op jit(solution)/shard_map/scatter | solution.py:151
  101.7 3.3 copy.127
  105.0 71.5 %all_to_all.10 = bf16[2,32,40,1024]{3,2,0,1:T(8,128)(2,1)S(1)} all-to-all(bf16[2,32,40,1024]{3,2,0,1:T(8,128)(2,1)S(1)} %copy.127), channel_id=1, replica_groups=mesh['req'=4,'exp'=32] {'exp'}, dimensions={1} | all-to-all | bytes 10485760 | tf_op jit(solution)/shard_map/all_to_all | solution.py:153
  176.5 8.2 %fusion.19 = f32[2,32,1,40,1024]{4,3,1,0,2:T(8,128)} fusion(bf16[2,1,1024,1024]{3,2,1,0:T(8,128)(2,1)S(1)} %copy-done.20, bf16[2,32,40,1024]{3,2,0,1:T(8,128)(2,1)S(1)} %all_to_all.10), kind=kOutput, calls=%fused_computation.34 | convolution fusion | flops 5368709120 | bytes 19922944 | tf_op jit(solution)/shard_map/mslcd,mldf->mslcf/dot_general | solution.py:161
  184.7 7.2 %convolution_convert_fusion = bf16[2,32,40,1024]{3,2,1,0:T(8,128)(2,1)S(1)} fusion(f32[2,32,1,40,1024]{4,3,1,0,2:T(8,128)} %fusion.19, bf16[2,1,512,1024]{3,2,1,0:T(8,128)(2,1)S(1)} %copy-done), kind=kOutput, calls=%fused_computation.35 | convolution fusion | flops 2694840320 | bytes 17825792 | tf_op jit(solution)/shard_map/mslcf,mlfd->mslcd/dot_general | solution.py:163
  191.8 3.2 copy.129
  195.0 5.0 all-to-all-start.1
  200.2 61.7 %all-to-all-done.1 = bf16[2,32,40,1024]{3,2,0,1:T(8,128)(2,1)} async-done(((bf16[2,32,40,1024]{3,2,0,1:T(8,128)(2,1)}), bf16[2,32,40,1024]{3,2,0,1:T(8,128)(2,1)}, u32[]{:S(2)}, u32[]{:S(2)}) %all-to-all-start.1) | async-done | bytes 5242912 | tf_op jit(solution)/shard_map/all_to_all | solution.py:166
  261.9 5.6 copy.130
  267.5 14.1 %gather_fusion.1 = bf16[2048,1024]{1,0:T(8,128)(2,1)} fusion(bf16[2560,1024]{1,0:T(8,128)(2,1)} %bitcast.231, s32[2048]{0:T(1024)S(1)} %broadcast_clamp_fusion), kind=kCustom, calls=%fused_computation.1 | custom fusion | bytes 8396800 | tf_op jit(solution)/shard_map/gather | solution.py:173
  281.6 4.8 fusion.8
  287.8 73.6 %all-gather.5.cloned.1.call-done = bf16[2,4096,1024]{2,1,0:T(8,128)(2,1)} async-done(((bf16[2,128,1024]{2,1,0:T(8,128)(2,1)}), bf16[2,4096,1024]{2,1,0:T(8,128)(2,1)}) %all-gather.5.cloned.1.call-update) | async-done | bytes 16777232 | tf_op jit(solution)/shard_map/all_gather | solution.py:184
  361.4 79.6 %while.35 = (s32[]{:T(128)}, f32[8,2,512]{2,1,0:T(2,128)S(1)}, f32[8,2,512]{2,1,0:T(2,128)}, f32[8,2,512]{2,1,0:T(2,128)}, s32[8]{0:T(128)S(1)}, /*index=5*/bf16...) while((s32[]{:T(128)}, f32[8,2,512]{2,1,0:T(2,128)S(1)}, ...), condition=%wide.region_20.21_spmd.clone, body=%wide.region_16.20_spmd.clone.sunk | while | flops 2423583744 | bytes 17480380 | solution.py:204
  362.7 6.0 fusion.161
  372.6 6.0 fusion.161
  382.6 6.0 fusion.161
  392.5 6.0 fusion.161
  402.5 6.0 fusion.161
  412.4 6.0 fusion.161
  422.4 6.0 fusion.161
  432.3 6.0 fusion.161
  442.4 40.9 %all-gather.11.cloned.1.call-done = f32[32,2,4096]{2,1,0:T(2,128)} async-done(((f32[1,2,4096]{2,1,0:T(2,128)}), f32[32,2,4096]{2,1,0:T(2,128)}) %all-gather.11.cloned.1.call-update) | async-done | bytes 1048592 | tf_op jit(solution)/shard_map/all_gather | solution.py:21
  484.0 43.5 %all-gather.9.cloned.1.call-done = f32[32,2,4096]{2,1,0:T(2,128)} async-done(((f32[1,2,4096]{2,1,0:T(2,128)}), f32[32,2,4096]{2,1,0:T(2,128)}) %all-gather.9.cloned.1.call-update) | async-done | bytes 1048592 | tf_op jit(solution)/shard_map/all_gather | solution.py:21
  528.2 43.4 %all-gather.7.cloned.1.call-done = f32[32,2,4096]{2,1,0:T(2,128)} async-done(((f32[1,2,4096]{2,1,0:T(2,128)}), f32[32,2,4096]{2,1,0:T(2,128)}) %all-gather.7.cloned.1.call-update) | async-done | bytes 1048592 | tf_op jit(solution)/shard_map/all_gather | solution.py:21
  572.4 27.7 %while.34 = (s32[]{:T(128)}, f32[2,4096]{1,0:T(2,128)S(1)}, f32[2,4096]{1,0:T(2,128)S(1)}, f32[2,4096]{1,0:T(2,128)S(1)}, f32[32,2,4096]{2,1,0:T(2,128)}, /*inde...) while((s32[]{:T(128)}, f32[2,4096]{1,0:T(2,128)S(1)}, ...), condition=%wide.region_22.23_spmd, body=%wide.region_21.22_spmd.sunk | while | flops 57349 | bytes 295059 | solution.py:27
  600.3 64.1 %all-reduce = f32[512]{0:T(512)S(1)} all-reduce(f32[512]{0:T(512)S(1)} %select_reduce_fusion.1), channel_id=2, replica_groups=mesh['req'=4,'exp'=32] {'req','exp'}, use_global_device_ids=true, to_apply=%region_25.26.clone | all-reduce | flops 512 | bytes 4096
  (211 shorter events, 91.7 us)
Async XLA Ops:
  7.2 177.5 %copy-start = (bf16[2,1,512,1024]{3,2,1,0:T(8,128)(2,1)S(1)}, bf16[2,1,512,1024]{3,2,1,0:T(8,128)(2,1)}, u32[]{:S(2)}) copy-start(bf16[2,1,512,1024]{3,2,1,0:T(8,128)(2,1)} %param.26) | copy-start | bytes 6291460
  9.3 5.2 copy-start.21
  12.4 1.0 copy-start.2
  14.9 0.6 copy-start.15
  24.7 1.0 copy-start.3
  25.7 6.6 copy-start.11
  25.7 7.2 %copy-start.8 = (s32[2,128,8]{1,2,0:T(8,128)S(1)}, s32[2,128,8]{1,2,0:T(8,128)}, u32[]{:S(2)}) copy-start(s32[2,128,8]{1,2,0:T(8,128)} %param.19) | copy-start | bytes 24580
  31.3 8.2 %copy-start.4 = (bf16[2,128,1024]{2,1,0:T(8,128)(2,1)S(1)}, bf16[2,128,1024]{2,1,0:T(8,128)(2,1)}, u32[]{:S(2)}) copy-start(bf16[2,128,1024]{2,1,0:T(8,128)(2,1)} %param.16) | copy-start | bytes 1572868
  39.4 5.0 copy-start.5
  41.6 5.9 copy-start.13
  63.3 5.6 copy-start.7
  63.3 24.2 %copy-start.6 = (s32[2,1024]{1,0:T(2,128)S(1)}, s32[2,1024]{1,0:T(2,128)}, u32[]{:S(2)}) copy-start(s32[2,1024]{1,0:T(2,128)} %eq.95) | copy-start | bytes 24580
  63.3 24.3 %copy-start.9 = (s32[2,128,8]{1,2,0:T(8,128)S(1)}, s32[2,128,8]{1,2,0:T(8,128)}, u32[]{:S(2)}) copy-start(s32[2,128,8]{1,2,0:T(8,128)} %broadcast_multiply_fusion.1) | copy-start | bytes 24580
  63.3 24.6 %copy-start.18 = (s32[2]{0:T(128)S(1)}, s32[2]{0:T(128)}, u32[]{:S(2)}) copy-start(s32[2]{0:T(128)} %iota_multiply_fusion) | copy-start | bytes 28
  105.0 71.5 %copy-start.20 = (bf16[2,1,1024,1024]{3,2,1,0:T(8,128)(2,1)S(1)}, bf16[2,1,1024,1024]{3,2,1,0:T(8,128)(2,1)}, u32[]{:S(2)}) copy-start(bf16[2,1,1024,1024]{3,2,1,0:T(8,128)(2,1)} %param.25) | copy-start | bytes 12582916
  195.0 5.0 copy-start.14
  195.0 66.9 %all-to-all-start.1 = ((bf16[2,32,40,1024]{3,2,0,1:T(8,128)(2,1)}), bf16[2,32,40,1024]{3,2,0,1:T(8,128)(2,1)}, u32[]{:S(2)}, u32[]{:S(2)}) async-start(bf16[2,32,40,1024]{3,2,0,1:T(8,128)(2,1)} %copy.129), calls=%async_computation.1 | async-start | bytes 10485760 | tf_op jit(solution)/shard_map/all_to_all | solution.py:166
  200.0 161.4 %all-gather.5.cloned.1.call-start = ((), (), s32[]{:S(2)}) async-start(), calls=%async_computation.2 | async-start | bytes 17301504 | tf_op jit(solution)/shard_map/all_gather | solution.py:184
  281.6 6.2 copy-start.12
  287.7 195.5 %all-gather.11.cloned.1.call-start = ((), (), s32[]{:S(2)}) async-start(), calls=%async_computation.5 | async-start | bytes 1081344 | tf_op jit(solution)/shard_map/all_gather | solution.py:21
  361.4 238.7 %copy-start.16 = (s32[128]{0:T(128)S(1)}, s32[128]{0:T(128)}, u32[]{:S(2)}) copy-start(s32[128]{0:T(128)} %copy-done.15) | copy-start | bytes 1540
  361.4 238.8 %copy-start.19 = (s32[4]{0:T(128)S(1)}, s32[4]{0:T(128)}, u32[]{:S(2)}) copy-start(s32[4]{0:T(128)} %param.21) | copy-start | bytes 52
  441.0 0.8 copy-start.10
  441.0 224.0 %copy-start.1 = (bf16[2,1,512,1024]{3,2,1,0:T(8,128)(2,1)S(1)}, bf16[2,1,512,1024]{3,2,1,0:T(8,128)(2,1)}, u32[]{:S(2)}) copy-start(bf16[2,1,512,1024]{3,2,1,0:T(8,128)(2,1)} %param.26) | copy-start | bytes 6291460
  441.0 86.4 %all-gather.9.cloned.1.call-start = ((), (), s32[]{:S(2)}) async-start(), calls=%async_computation.4 | async-start | bytes 1081344 | tf_op jit(solution)/shard_map/all_gather | solution.py:21
  441.8 129.8 %all-gather.7.cloned.1.call-start = ((), (), s32[]{:S(2)}) async-start(), calls=%async_computation.3 | async-start | bytes 1081344 | tf_op jit(solution)/shard_map/all_gather | solution.py:21
  600.1 65.0 %copy-start.17 = (f32[2,128]{1,0:T(2,128)}, f32[2,128]{1,0:T(2,128)S(1)}, u32[]{:S(2)}) copy-start(f32[2,128]{1,0:T(2,128)S(1)} %add_subtract_fusion) | copy-start | bytes 3076
Sparse Core Ops, SparseCore 0:
  287.8 73.5 all-gather.4
  441.2 42.0 all-gather.10
  485.5 41.9 all-gather.8
  529.6 41.9 all-gather.6
where the time goes:
time: 675 us; the launch traced here: 672 us
  waiting for transfers between devices  264 us (39%)
  blocking collectives  136 us (20%)
  matrix products  88 us (13%)
  local copies, waits for them, and re-layouts  84.9 us (13%)
  other arithmetic  73.5 us (11%)
  between operations  14.3 us (2%)
    all_gather x3, waiting for transfers between devices, combined_all(): everything = jax.tree.map(lambda part: lax.all_gather(part, axis), x)  128 us
    all_gather x1, waiting for transfers between devices, per_device(): shard_piece = lax.all_gather(final, 'exp', axis=1, tiled=True)  73.6 us
    all_to_all x1, blocking collectives, per_device(): lax.all_to_all(outgoing.reshape(2, groups, local_count * CAP, width), 'ex...  71.5 us
    unnamed x1, blocking collectives  64.1 us
    all_to_all x1, waiting for transfers between devices, per_device(): lax.all_to_all(produced.reshape(2, groups, local_count * CAP, width), 'ex...  61.7 us
    dot_general x8, matrix products, one_block(): jnp.einsum('mtd,mvd->mtv', row_block, vocab_head, preferred_element_type=...  47.9 us
    add x31, other arithmetic, join_parts(): first_mass * jnp.exp(first_max - joined_max)  27.2 us
    gather x2, local copies, waits for them, and re-layouts, per_device(): moe_in[:, token_index].reshape(-1, width)  21.3 us
  transfers between devices with their start and end apart: 5, of which 5 were waited for; matrix products, arithmetic and copies ran while one was open for 0% of the time, Pallas kernels for 0%

commit v1 on v0

--- a/solution.py
+++ b/solution.py
@@ -181,7 +181,17 @@
     vocab_rows = vocab_head.shape[1]
     lowest = shard * vocab_rows
     vocab_ids = jnp.arange(vocab_rows, dtype=jnp.int32)
-    shard_piece = lax.all_gather(final, "exp", axis=1, tiled=True)
+
+    def report_circles_all(frame):
+        state_next = lax.all_to_all(
+            jnp.stack([frame for _ in range(lax.axis_size("exp"))]),
+            axis_name="exp",
+            split_axis=0,
+            concat_axis=0,
+        )
+        return jnp.concatenate(state_next, 1)
+
+    shard_piece = report_circles_all(final)
     piece_rows = shard_piece.shape[1]
     block_rows = 512
     block_count = piece_rows // block_rows

time: 675 us -> 840 us (1.24)
  waiting for transfers between devices: 264 us -> 401 us
  local copies, waits for them, and re-layouts: 84.9 us -> 105 us
  starting transfers between devices: 5.14 us -> 14.4 us
    all_to_all x0 -> x1, waiting for transfers between devices: none -> 201 us  [report_circles_all(): lax.all_to_all(jnp.stack([frame for _ in range(lax.axis_size('exp'))]), a...]
    all_gather x1 -> x0, waiting for transfers between devices: 73.6 us -> none  [per_device(): shard_piece = lax.all_gather(final, 'exp', axis=1, tiled=True)]
    all_to_all x0 -> x1, local copies, waits for them, and re-layouts: none -> 13.9 us  [report_circles_all(): lax.all_to_all(jnp.stack([frame for _ in range(lax.axis_size('exp'))]), a...]
    all_to_all x0 -> x1, starting transfers between devices: none -> 9.25 us  [report_circles_all(): lax.all_to_all(jnp.stack([frame for _ in range(lax.axis_size('exp'))]), a...]
    all_gather x3, waiting for transfers between devices: 128 us -> 137 us  [combined_all(): everything = jax.tree.map(lambda part: lax.all_gather(part, axis), x)]
where the time goes in v1:
time: 840 us; the launch traced here: 837 us
  waiting for transfers between devices  401 us (48%)
  blocking collectives  136 us (16%)
  local copies, waits for them, and re-layouts  105 us (12%)
  matrix products  88.1 us (10%)
  other arithmetic  72.7 us (9%)
  starting transfers between devices  14.4 us (2%)
  between operations  14.3 us (2%)
    all_to_all x1, waiting for transfers between devices, report_circles_all(): lax.all_to_all(jnp.stack([frame for _ in range(lax.axis_size('exp'))]), a...  201 us
    all_gather x3, waiting for transfers between devices, combined_all(): everything = jax.tree.map(lambda part: lax.all_gather(part, axis), x)  137 us
    all_to_all x1, blocking collectives, per_device(): lax.all_to_all(outgoing.reshape(2, groups, local_count * CAP, width), 'ex...  71.5 us
    unnamed x1, blocking collectives  64.1 us
    all_to_all x1, waiting for transfers between devices, per_device(): lax.all_to_all(produced.reshape(2, groups, local_count * CAP, width), 'ex...  61.8 us
    dot_general x8, matrix products, one_block(): jnp.einsum('mtd,mvd->mtv', row_block, vocab_head, preferred_element_type=...  47.9 us
    add x31, other arithmetic, join_parts(): first_mass * jnp.exp(first_max - joined_max)  27.2 us
    gather x2, local copies, waits for them, and re-layouts, per_device(): moe_in[:, token_index].reshape(-1, width)  21.3 us
  transfers between devices with their start and end apart: 5, of which 5 were waited for; matrix products, arithmetic and copies ran while one was open for 0% of the time, Pallas kernels for 0%

profile of v1, /device:TPU:1, one launch (start us, length us, event | category | flops | bytes accessed | tf_op | source)
XLA Modules:
  0.0 836.9 jit_solution(8522667930521256179)
XLA Ops:
  47.5 15.8 %gather_fusion = bf16[1024,2,1024]{2,1,0:T(2,128)(2,1)} fusion(bf16[2,128,1024]{2,0,1:T(2,128)(2,1)S(1)} %copy.126, s32[1024]{0:T(1024)S(1)} %broadcast_clamp_fusion.1), kind=kCustom, calls=%fused_computation | custom fusion | bytes 8392704 | tf_op jit(solution)/shard_map/gather | solution.py:151
  63.3 5.6 copy.127
  68.8 18.0 %reduce-window.11 = s32[2,32,8,128]{3,2,1,0:T(8,128)S(1)} reduce-window(s32[2,32,8,128]{3,2,1,0:T(8,128)S(1)} %fusion.101, s32[]{:T(128)} %constant.119.clone.1), window={size=1x1x1x128 pad=0_0x0_0x0_0x127_0}, to_apply=%region_9.10 | reduce-window | flops 8323072 | bytes 524292 | tf_op jit(solution)/shard_map/reduce-window.1
  88.0 13.6 %scatter_custom_fusion = bf16[2560,1024]{1,0:T(8,128)(2,1)} fusion(s32[2048]{0:T(1024)S(1)} %bitcast.266, bf16[2048,1024]{1,0:T(8,128)(2,1)} %bitcast.244, bf16[]{:T(256)} %constant.129.clone.1), kind=kCustom, calls=%fused_computation.37 | custom fusion | bytes 5243392 | tf_op jit(solution)/shard_map/scatter | solution.py:151
  101.6 3.3 copy.128
  104.9 71.5 %all_to_all.15 = bf16[2,32,40,1024]{3,2,0,1:T(8,128)(2,1)S(1)} all-to-all(bf16[2,32,40,1024]{3,2,0,1:T(8,128)(2,1)S(1)} %copy.128), channel_id=1, replica_groups=mesh['req'=4,'exp'=32] {'exp'}, dimensions={1} | all-to-all | bytes 10485760 | tf_op jit(solution)/shard_map/all_to_all | solution.py:153
  176.4 8.2 fusion.19
  184.6 7.2 convolution_convert_fusion
  191.8 3.2 copy.130
  195.0 5.0 all-to-all-start.1
  200.1 61.8 %all-to-all-done.1 = bf16[2,32,40,1024]{3,2,0,1:T(8,128)(2,1)} async-done(((bf16[2,32,40,1024]{3,2,0,1:T(8,128)(2,1)}), bf16[2,32,40,1024]{3,2,0,1:T(8,128)(2,1)}, u32[]{:S(2)}, u32[]{:S(2)}) %all-to-all-start.1) | async-done | bytes 5242912 | tf_op jit(solution)/shard_map/all_to_all | solution.py:166
  261.9 5.6 copy.131
  267.4 14.1 %gather_fusion.1 = bf16[2048,1024]{1,0:T(8,128)(2,1)} fusion(bf16[2560,1024]{1,0:T(8,128)(2,1)} %bitcast.234, s32[2048]{0:T(1024)S(1)} %broadcast_clamp_fusion), kind=kCustom, calls=%fused_computation.1 | custom fusion | bytes 8396800 | tf_op jit(solution)/shard_map/gather | solution.py:173
  281.6 4.8 fusion.8
  286.8 6.0 stack.11
  292.8 9.3 %all-to-all-start.2 = ((bf16[32,2,128,1024]{3,2,1,0:T(8,128)(2,1)}), bf16[32,2,128,1024]{3,2,1,0:T(8,128)(2,1)}, u32[]{:S(2)}, u32[]{:S(2)}) async-start(bf16[32,2,128,1024]{3,2,1,0:T(8,128)(2,1)} %stack.11), calls=%async_computation.2 | async-start | bytes 33554432 | tf_op jit(solution)/shard_map/all_to_all | solution.py:186
  302.2 201.5 %all-to-all-done.2 = bf16[32,2,128,1024]{3,2,1,0:T(8,128)(2,1)} async-done(((bf16[32,2,128,1024]{3,2,1,0:T(8,128)(2,1)}), bf16[32,2,128,1024]{3,2,1,0:T(8,128)(2,1)}, u32[]{:S(2)}, u32[]{:S(2)}) %all-to-all-start.2) | async-done | bytes 16777248 | tf_op jit(solution)/shard_map/all_to_all | solution.py:186
  503.7 13.9 %copy.132 = bf16[32,2,128,1024]{3,2,0,1:T(8,128)(2,1)} copy(bf16[32,2,128,1024]{3,2,1,0:T(8,128)(2,1)} %all-to-all-done.2) | data formatting | bytes 33554432 | tf_op jit(solution)/shard_map/all_to_all | solution.py:186
  517.6 79.6 %while.35 = (s32[]{:T(128)}, f32[8,2,512]{2,1,0:T(2,128)S(1)}, f32[8,2,512]{2,1,0:T(2,128)}, f32[8,2,512]{2,1,0:T(2,128)}, s32[8]{0:T(128)S(1)}, /*index=5*/bf16...) while((s32[]{:T(128)}, f32[8,2,512]{2,1,0:T(2,128)S(1)}, ...), condition=%wide.region_20.21_spmd.clone, body=%wide.region_16.20_spmd.clone.sunk | while | flops 2423583744 | bytes 17480380 | solution.py:214
  518.8 6.0 fusion.161
  528.8 6.0 fusion.161
  538.7 6.0 fusion.161
  548.7 6.0 fusion.161
  558.6 6.0 fusion.161
  568.5 6.0 fusion.161
  578.5 6.0 fusion.161
  588.4 6.0 fusion.161
  598.7 49.8 %all-gather.8.cloned.1.call-done = f32[32,2,4096]{2,1,0:T(2,128)} async-done(((f32[1,2,4096]{2,1,0:T(2,128)}), f32[32,2,4096]{2,1,0:T(2,128)}) %all-gather.8.cloned.1.call-update) | async-done | bytes 1048592 | tf_op jit(solution)/shard_map/all_gather | solution.py:21
  649.2 43.5 %all-gather.6.cloned.1.call-done = f32[32,2,4096]{2,1,0:T(2,128)} async-done(((f32[1,2,4096]{2,1,0:T(2,128)}), f32[32,2,4096]{2,1,0:T(2,128)}) %all-gather.6.cloned.1.call-update) | async-done | bytes 1048592 | tf_op jit(solution)/shard_map/all_gather | solution.py:21
  693.4 43.5 %all-gather.4.cloned.1.call-done = f32[32,2,4096]{2,1,0:T(2,128)} async-done(((f32[1,2,4096]{2,1,0:T(2,128)}), f32[32,2,4096]{2,1,0:T(2,128)}) %all-gather.4.cloned.1.call-update) | async-done | bytes 1048592 | tf_op jit(solution)/shard_map/all_gather | solution.py:21
  737.7 27.7 %while.34 = (s32[]{:T(128)}, f32[2,4096]{1,0:T(2,128)S(1)}, f32[2,4096]{1,0:T(2,128)S(1)}, f32[2,4096]{1,0:T(2,128)S(1)}, f32[32,2,4096]{2,1,0:T(2,128)}, /*inde...) while((s32[]{:T(128)}, f32[2,4096]{1,0:T(2,128)S(1)}, ...), condition=%wide.region_22.23_spmd, body=%wide.region_21.22_spmd.sunk | while | flops 57349 | bytes 295059 | solution.py:27
  765.6 64.1 %all-reduce = f32[512]{0:T(512)S(1)} all-reduce(f32[512]{0:T(512)S(1)} %select_reduce_fusion.1), channel_id=2, replica_groups=mesh['req'=4,'exp'=32] {'req','exp'}, use_global_device_ids=true, to_apply=%region_25.26.clone | all-reduce | flops 512 | bytes 4096
  (212 shorter events, 99.8 us)
Async XLA Ops:
  7.2 177.4 %copy-start = (bf16[2,1,512,1024]{3,2,1,0:T(8,128)(2,1)S(1)}, bf16[2,1,512,1024]{3,2,1,0:T(8,128)(2,1)}, u32[]{:S(2)}) copy-start(bf16[2,1,512,1024]{3,2,1,0:T(8,128)(2,1)} %param.26) | copy-start | bytes 6291460
  9.3 5.2 copy-start.21
  12.4 1.0 copy-start.2
  14.9 0.5 copy-start.15
  24.6 1.0 copy-start.3
  25.6 6.6 copy-start.11
  25.6 7.2 copy-start.8
  31.2 8.2 copy-start.4
  39.4 5.0 copy-start.5
  41.6 5.9 copy-start.13
  63.2 5.6 copy-start.7
  63.3 24.2 %copy-start.6 = (s32[2,1024]{1,0:T(2,128)S(1)}, s32[2,1024]{1,0:T(2,128)}, u32[]{:S(2)}) copy-start(s32[2,1024]{1,0:T(2,128)} %eq.95) | copy-start | bytes 24580
  63.3 24.3 %copy-start.9 = (s32[2,128,8]{1,2,0:T(8,128)S(1)}, s32[2,128,8]{1,2,0:T(8,128)}, u32[]{:S(2)}) copy-start(s32[2,128,8]{1,2,0:T(8,128)} %broadcast_multiply_fusion.1) | copy-start | bytes 24580
  63.3 24.6 %copy-start.18 = (s32[2]{0:T(128)S(1)}, s32[2]{0:T(128)}, u32[]{:S(2)}) copy-start(s32[2]{0:T(128)} %iota_multiply_fusion) | copy-start | bytes 28
  104.9 71.5 %copy-start.20 = (bf16[2,1,1024,1024]{3,2,1,0:T(8,128)(2,1)S(1)}, bf16[2,1,1024,1024]{3,2,1,0:T(8,128)(2,1)}, u32[]{:S(2)}) copy-start(bf16[2,1,1024,1024]{3,2,1,0:T(8,128)(2,1)} %param.25) | copy-start | bytes 12582916
  195.0 5.0 copy-start.14
  195.0 66.9 %all-to-all-start.1 = ((bf16[2,32,40,1024]{3,2,0,1:T(8,128)(2,1)}), bf16[2,32,40,1024]{3,2,0,1:T(8,128)(2,1)}, u32[]{:S(2)}, u32[]{:S(2)}) async-start(bf16[2,32,40,1024]{3,2,0,1:T(8,128)(2,1)} %copy.130), calls=%async_computation.1 | async-start | bytes 10485760 | tf_op jit(solution)/shard_map/all_to_all | solution.py:166
  292.8 9.4 %copy-start.12 = (s32[4096]{0:T(1024)S(1)}, s32[4096]{0:T(1024)}, u32[]{:S(2)}) copy-start(s32[4096]{0:T(1024)} %param.18) | copy-start | bytes 49156
  292.8 210.8 %all-to-all-start.2 = ((bf16[32,2,128,1024]{3,2,1,0:T(8,128)(2,1)}), bf16[32,2,128,1024]{3,2,1,0:T(8,128)(2,1)}, u32[]{:S(2)}, u32[]{:S(2)}) async-start(bf16[32,2,128,1024]{3,2,1,0:T(8,128)(2,1)} %stack.11), calls=%async_computation.2 | async-start | bytes 33554432 | tf_op jit(solution)/shard_map/all_to_all | solution.py:186
  302.1 346.3 %all-gather.8.cloned.1.call-start = ((), (), s32[]{:S(2)}) async-start(), calls=%async_computation.5 | async-start | bytes 1081344 | tf_op jit(solution)/shard_map/all_gather | solution.py:21
  517.6 247.9 %copy-start.16 = (s32[128]{0:T(128)S(1)}, s32[128]{0:T(128)}, u32[]{:S(2)}) copy-start(s32[128]{0:T(128)} %copy-done.15) | copy-start | bytes 1540
  517.6 248.0 %copy-start.19 = (s32[4]{0:T(128)S(1)}, s32[4]{0:T(128)}, u32[]{:S(2)}) copy-start(s32[4]{0:T(128)} %param.21) | copy-start | bytes 52
  597.1 0.8 copy-start.10
  597.1 233.2 %copy-start.1 = (bf16[2,1,512,1024]{3,2,1,0:T(8,128)(2,1)S(1)}, bf16[2,1,512,1024]{3,2,1,0:T(8,128)(2,1)}, u32[]{:S(2)}) copy-start(bf16[2,1,512,1024]{3,2,1,0:T(8,128)(2,1)} %param.26) | copy-start | bytes 6291460
  597.2 95.5 %all-gather.6.cloned.1.call-start = ((), (), s32[]{:S(2)}) async-start(), calls=%async_computation.4 | async-start | bytes 1081344 | tf_op jit(solution)/shard_map/all_gather | solution.py:21
  597.9 139.0 %all-gather.4.cloned.1.call-start = ((), (), s32[]{:S(2)}) async-start(), calls=%async_computation.3 | async-start | bytes 1081344 | tf_op jit(solution)/shard_map/all_gather | solution.py:21
  765.4 65.0 %copy-start.17 = (f32[2,128]{1,0:T(2,128)}, f32[2,128]{1,0:T(2,128)S(1)}, u32[]{:S(2)}) copy-start(f32[2,128]{1,0:T(2,128)S(1)} %add_subtract_fusion) | copy-start | bytes 3076
Sparse Core Ops, SparseCore 0:
  597.3 51.0 all-gather.7
  650.7 41.9 all-gather.5
  694.9 41.9 all-gather.3
